TPU v7x, 256 devices: a whole 4x4x8 slice. The times are simulated.
256 devices in a mesh: section: 16 (over y_lo, x, core), expert: 16 (over z, y_hi).
Axes of the slice: x: 4, y: 4 (y_hi: 2, y_lo: 2; y = y_hi * 2 + y_lo), z: 8, core: 2. Of those that a mesh axis runs over, the one named last changes fastest.
Arguments:
- activations: bfloat16 [16384, 8192], P('section', 'expert'), may hold values from -12 to 12
- modality: int32 [16384], P('section'), may hold values from 0 to 1
- selected: int32 [16, 256], P('section'), may hold values from 0 to 1023, as said below
- routes: int32 [4096, 1], P('section'), may hold values from 0 to 15, as said below
- norm_gain: float32 [2, 8192], P(None, 'expert'), may hold values from 0.1 to 1.9
- router: float32 [8192], P('expert'), may hold values from -0.0625 to 0.0625
- gate_w: bfloat16 [16, 3072, 8192], P('expert', 'section'), may hold values from -0.0625 to 0.0625
- up_w: bfloat16 [16, 3072, 8192], P('expert', 'section'), may hold values from -0.0625 to 0.0625
- down_w: bfloat16 [16, 3072, 8192], P('expert', 'section'), may hold values from -0.21875 to 0.21875
Outputs:
- block_out: bfloat16 [16384, 8192], P('section', 'expert')
Inputs may be any that keep to these rules, and one draw needn't show every extreme that they name: Each row of selected lists 256 different positions in rising order, the first and the last position among them. `routes`: among the 256 rows of one section group no expert is named more than 24 times, and some expert exactly 24 times; the entry for selected[s, j] is below 8 if that token's modality is 0, and 8 or more if it is 1.
All inputs are finite; a program needn't handle non-finite values.
Results may differ from a plain program's by a relative error of at most 0.0075.
Values may be sent and summed in bfloat16 or wider, within the bound.
No kernel may reach another device: no remote copies, remote signals or barrier semaphores. Data moves between devices by JAX's collectives and lax.ppermute only.
A program may use at most 128 MiB of HBM per device.

v0:
```python
import jax
import jax.numpy as jnp
from jax import lax
from jax.sharding import PartitionSpec as P

EPS = 1e-05


def passed_along(block, axis, distance):
    devices = range(lax.axis_size(axis))
    route = [((i - distance) % len(devices), i) for i in devices]
    return lax.ppermute(block, axis, route)


def feature_product(block, weight):
    return lax.dot_general(
        block, weight, (((1,), (1,)), ((), ())), preferred_element_type=jnp.float32
    )


def slots_of(experts, expert_count):
    onehot = (experts[:, None] == jnp.arange(expert_count, dtype=jnp.int32)[None, :]).astype(
        jnp.int32
    )
    ranks = jnp.cumsum(onehot, axis=0) - 1
    return jnp.sum(ranks * onehot, axis=1)


def body(activations, modality, selected, routes, norm_gain, router, gate_w, up_w, down_w):
    n_section = lax.axis_size("section")
    sel_count = selected.shape[1]
    expert_count = lax.axis_size("expert") * gate_w.shape[0]
    capacity = max(2, 3 * sel_count // (2 * expert_count))
    groups = n_section
    arrived = passed_along(activations, "section", 1)
    sel_next = passed_along(selected, "section", -1)[0]
    routes_next = passed_along(routes, "section", -1)[:, 0]
    rows = activations[sel_next]
    target = routes_next * capacity + slots_of(routes_next, expert_count)
    placing = (
        target[None, :] == jnp.arange(expert_count * capacity, dtype=jnp.int32)[:, None]
    ).astype(jnp.bfloat16)
    feature_width = rows.shape[1]
    buffer = jnp.dot(placing, rows, preferred_element_type=jnp.float32).astype(jnp.bfloat16)
    buffer = buffer.reshape(expert_count, capacity, feature_width)
    n_exp_dev = lax.axis_size("expert")
    local_width = router.shape[0]
    tables = jnp.concatenate([norm_gain, router[None, :]], axis=0)
    parts = []
    rest = tables
    for _ in range(3):
        piece = rest.astype(jnp.bfloat16)
        parts.append(piece)
        rest = rest - piece.astype(jnp.float32)
    table_rows = tables.shape[0]
    extra = jnp.broadcast_to(
        jnp.concatenate(parts, axis=0)[None], (expert_count, 3 * table_rows, local_width)
    )
    buffer = jnp.concatenate([buffer, extra], axis=1)
    mine = lax.all_to_all(buffer, "expert", split_axis=0, concat_axis=2, tiled=True)[0]
    arrived, mine = lax.optimization_barrier((arrived, mine))
    coded = mine[capacity:].astype(jnp.float32).reshape(3, table_rows, mine.shape[1])
    tables = coded[0] + coded[1] + coded[2]
    mine = mine[:capacity]
    gains_all = tables[:2]
    router_all = tables[2]
    expert_id = lax.axis_index("expert")
    kind = (expert_id >= expert_count // 2).astype(jnp.int32)
    gains = lax.dynamic_index_in_dim(gains_all, kind, axis=0, keepdims=False)
    picked = mine.astype(jnp.float32)
    d = picked.shape[1]
    scale = lax.rsqrt(jnp.sum(picked * picked, axis=1) / d + EPS)
    normed = (picked * scale[:, None] * gains[None, :]).astype(jnp.bfloat16)
    score = jax.nn.sigmoid(scale * jnp.sum(picked * gains[None, :] * router_all[None, :], axis=1))
    score_home = passed_along(score, "section", 1)
    half = d // 2
    block_a = lax.all_gather(normed[:, :half], "section", axis=0, tiled=True)
    block_b = lax.all_gather(normed[:, half:], "section", axis=0, tiled=True)
    block_a, score_home = lax.optimization_barrier((block_a, score_home))
    gate = feature_product(block_a, gate_w[0, :, :half]) + feature_product(
        block_b, gate_w[0, :, half:]
    )
    upper = feature_product(block_a, up_w[0, :, :half]) + feature_product(
        block_b, up_w[0, :, half:]
    )
    hidden = (jax.nn.silu(gate) * upper).astype(jnp.bfloat16)
    hidden_width = hidden.shape[1]
    hidden = jnp.roll(hidden.reshape(groups, capacity, hidden_width), 1, axis=0).reshape(
        groups * capacity, hidden_width
    )
    pieces = []
    for columns in (slice(0, half), slice(half, d)):
        part = jnp.dot(hidden, down_w[0, :, columns], preferred_element_type=jnp.float32)
        pieces.append(
            lax.psum_scatter(
                lax.optimization_barrier(part.astype(jnp.bfloat16))
                .astype(jnp.float32)
                .astype(jnp.bfloat16),
                "section",
                scatter_dimension=0,
                tiled=True,
            )
        )
    summed = jnp.concatenate(pieces, axis=1)
    update_rows = (score_home[:, None] * summed.astype(jnp.float32)).astype(jnp.bfloat16)
    outgoing = update_rows.reshape(capacity, n_exp_dev, local_width).transpose(1, 0, 2)
    back = lax.all_to_all(outgoing, "expert", split_axis=0, concat_axis=0, tiled=True)
    flat_back = back.reshape(expert_count * capacity, local_width)
    picks = selected[0]
    experts = routes[:, 0]
    position = experts * capacity + slots_of(experts, expert_count)
    update = flat_back[position].astype(jnp.float32)
    result = arrived.astype(jnp.float32).at[picks].add(update)
    return result.astype(jnp.bfloat16)


def solution(mesh):
    placed = (
        P("section", "expert"),
        P("section"),
        P("section", None),
        P("section", None),
        P(None, "expert"),
        P("expert"),
        P("expert", "section", None),
        P("expert", "section", None),
        P("expert", "section", None),
    )
    return jax.shard_map(
        body, mesh=mesh, in_specs=placed, out_specs=P("section", "expert"), check_vma=False
    )
```

profile of v0, /device:TPU:7, one launch (start us, length us, event | category | flops | bytes accessed | tf_op | source)
XLA Modules:
  0.0 310.3 jit_solution(3256144085192003870)
XLA Ops:
  6.5 0.7 collective-permute-start.1
  7.2 0.3 collective-permute-start.2
  7.5 3.6 %collective-permute-start = (bf16[1024,512]{1,0:T(8,128)(2,1)}, bf16[1024,512]{1,0:T(8,128)(2,1)S(1)}, u32[]{:S(2)}, u32[]{:S(2)}) collective-permute-start(bf16[1024,512]{1,0:T(8,128)(2,1)} %param.9), channel_id=1, source_target_pairs={{240,0},{0,16},{16,32},{32,48},{48,64},{64,80},{80,96},{96,112},{1... | collective-permute-start | bytes 3145736 | tf_op jit(solution)/shard_map/ppermute | solution.py:12
  11.1 0.7 fusion.38
  11.8 0.7 fusion.37
  12.5 0.0 collective-permute-done.1
  12.5 0.6 reduce-window.14
  13.1 0.2 slice_reduce_fusion.1
  13.4 0.1 fusion.34
  13.5 0.0 collective-permute-done.2
  13.5 2.6 gather_fusion
  16.1 0.3 convolution_convert_fusion.2
  16.4 0.9 pad_maximum_fusion
  17.3 10.9 %all-to-all-start = ((bf16[16,33,512]{2,1,0:T(8,128)(2,1)}), bf16[16,33,512]{2,1,0:T(8,128)(2,1)S(1)}, u32[]{:S(2)}, u32[]{:S(2)}) async-start(bf16[16,33,512]{2,1,0:T(8,128)(2,1)} %pad_maximum_fusion), calls=%async_computation | async-start | bytes 1310720 | tf_op jit(solution)/shard_map/all_to_all | solution.py:60
  28.2 0.0 all-gather.3.cloned.1.call-start
  28.3 19.4 %all-to-all-done = bf16[16,33,512]{2,1,0:T(8,128)(2,1)S(1)} async-done(((bf16[16,33,512]{2,1,0:T(8,128)(2,1)}), bf16[16,33,512]{2,1,0:T(8,128)(2,1)S(1)}, u32[]{:S(2)}, u32[]{:S(2)}) %all-to-all-start) | async-done | bytes 540704 | tf_op jit(solution)/shard_map/all_to_all | solution.py:60
  47.6 0.2 copy.34
  47.8 0.1 pad.13
  47.9 0.4 copy.28
  48.3 0.0 collective-permute-done
  48.3 0.0 copy-start.1
  48.3 0.1 slice_add_fusion
  48.5 0.3 fusion.26
  48.8 0.2 fusion.24
  49.0 0.8 fusion.40
  49.8 0.0 all-gather.3.cloned.1.call-update
  49.8 0.0 all-gather.5.cloned.1.call-start
  49.9 0.7 all-gather.5.cloned.1.call-update
  50.6 0.0 reduce-scatter.3.cloned.1.call-start
  50.6 2.0 collective-permute-start.3
  52.6 0.7 collective-permute-done.3
  53.4 29.1 %all-gather.3.cloned.1.call-done = bf16[384,4096]{1,0:T(8,128)(2,1)} async-done(((bf16[24,4096]{1,0:T(8,128)(2,1)}), bf16[384,4096]{1,0:T(8,128)(2,1)}) %all-gather.3.cloned.1.call-update) | async-done | bytes 3145744 | tf_op jit(solution)/shard_map/all_gather | solution.py:77
  82.5 40.4 %all-gather.5.cloned.1.call-done = bf16[384,4096]{1,0:T(8,128)(2,1)} async-done(((bf16[24,4096]{1,0:T(8,128)(2,1)}), bf16[384,4096]{1,0:T(8,128)(2,1)}) %all-gather.5.cloned.1.call-update) | async-done | bytes 3145744 | tf_op jit(solution)/shard_map/all_gather | solution.py:78
  122.9 3.7 %fusion.6 = f32[384,192]{0,1:T(8,128)S(1)} fusion(bf16[384,4096]{1,0:T(8,128)(2,1)} %all-gather.5.cloned.1.call-done, bf16[1,192,8192]{2,1,0:T(8,128)(2,1)} %param.14), kind=kOutput, calls=%fused_computation.11 | convolution fusion | flops 603979776 | bytes 5013504 | tf_op jit(solution)/shard_map/dot_general | solution.py:16
  126.6 0.0 copy-start.6
  126.6 3.2 %fusion.16 = f32[384,192]{0,1:T(8,128)S(1)} fusion(f32[384,192]{0,1:T(8,128)S(1)} %fusion.6, bf16[384,4096]{1,0:T(8,128)(2,1)} %all-gather.3.cloned.1.call-done, bf16[1,192,8192]{2,1,0:T(8,128)(2,1)S(1)} %copy-done.5), kind=kOutput, calls=%fused_computation.25 | convolution fusion | flops 604053504 | bytes 5308416 | tf_op jit(solution)/shard_map/dot_general | solution.py:16
  129.9 0.0 copy-done.8
  129.9 1.2 fusion.2
  131.1 0.7 copy-done.7
  131.8 1.2 multiply_convert_fusion.1
  133.0 0.1 slice_bitcast_fusion
  133.1 0.1 copy.19
  133.3 0.1 copy.20
  133.3 0.1 pad_maximum_fusion.1
  133.4 0.3 copy-done
  133.7 2.7 convolution_convert_fusion.1
  136.4 0.0 reduce-scatter.3.cloned.1.call-update
  136.4 0.0 copy-start.3
  136.4 0.2 reduce-scatter.5.cloned.1.call-start
  136.6 2.6 convolution_convert_fusion
  139.3 0.0 reduce-scatter.5.cloned.1.call-update
  139.3 0.6 reduce-window.16
  139.9 63.1 %reduce-scatter.3.cloned.1.call-done = bf16[24,4096]{1,0:T(8,128)(2,1)} async-done(((bf16[384,4096]{1,0:T(8,128)(2,1)}), bf16[24,4096]{1,0:T(8,128)(2,1)}) %reduce-scatter.3.cloned.1.call-update) | async-done | bytes 196624 | tf_op jit(solution)/shard_map/reduce_scatter | solution.py:95
  203.1 0.9 copy.36
  204.0 67.6 %reduce-scatter.5.cloned.1.call-done = bf16[24,4096]{1,0:T(8,128)(2,1)} async-done(((bf16[384,4096]{1,0:T(8,128)(2,1)}), bf16[24,4096]{1,0:T(8,128)(2,1)}) %reduce-scatter.5.cloned.1.call-update) | async-done | bytes 196624 | tf_op jit(solution)/shard_map/reduce_scatter | solution.py:95
  271.6 0.9 copy.35
  272.6 0.9 fusion.29
  273.5 9.1 %all-to-all-start.1 = ((bf16[16,24,512]{2,1,0:T(8,128)(2,1)}), bf16[16,24,512]{2,1,0:T(8,128)(2,1)S(1)}, u32[]{:S(2)}, u32[]{:S(2)}) async-start(bf16[16,24,512]{2,1,0:T(8,128)(2,1)} %fusion.29), calls=%async_computation.3 | async-start | bytes 786432 | tf_op jit(solution)/shard_map/all_to_all | solution.py:107
  282.6 0.2 slice_reduce_fusion
  282.8 0.1 fusion.32
  283.0 0.3 convert_element_type.78
  283.2 15.4 %all-to-all-done.1 = bf16[16,24,512]{2,1,0:T(8,128)(2,1)S(1)} async-done(((bf16[16,24,512]{2,1,0:T(8,128)(2,1)}), bf16[16,24,512]{2,1,0:T(8,128)(2,1)S(1)}, u32[]{:S(2)}, u32[]{:S(2)}) %all-to-all-start.1) | async-done | bytes 393248 | tf_op jit(solution)/shard_map/all_to_all | solution.py:107
  298.6 4.0 %scatter_custom_fusion = f32[1024,512]{1,0:T(8,128)S(1)} fusion(f32[1024,512]{1,0:T(8,128)S(1)} %convert_element_type.78, s32[256]{0:T(256)S(1)} %bitcast.131, bf16[384,512]{1,0:T(8,128)(2,1)S(1)} %bitcast.110, s32[1024]{0:T(1024)S(1)} %pad_clamp_fusion), kind=kCustom, calls=%fused_computation.35 | custom fusion | flops 262144 | bytes 2494464 | tf_op jit(solution)/shard_map/scatter-add | solution.py:113
  302.7 1.1 convert_element_type.90
  (31 shorter events, 0.3 us)
Async XLA Ops:
  6.5 6.0 %collective-permute-start.1 = (s32[256,1]{0,1:T(1,128)}, s32[256,1]{0,1:T(1,128)S(1)}, u32[]{:S(2)}, u32[]{:S(2)}) collective-permute-start(s32[256,1]{0,1:T(1,128)} %param.11), channel_id=1, source_target_pairs={{16,0},{32,16},{48,32},{64,48},{80,64},{96,80},{112,96},{128,112},... | collective-permute-start | bytes 3080 | tf_op jit(solution)/shard_map/ppermute | solution.py:12
  7.2 6.2 %collective-permute-start.2 = (s32[1,256]{1,0:T(1,128)}, s32[1,256]{1,0:T(1,128)S(1)}, u32[]{:S(2)}, u32[]{:S(2)}) collective-permute-start(s32[1,256]{1,0:T(1,128)} %param.10), channel_id=1, source_target_pairs={{16,0},{32,16},{48,32},{64,48},{80,64},{96,80},{112,96},{128,112},... | collective-permute-start | bytes 3080 | tf_op jit(solution)/shard_map/ppermute | solution.py:12
  7.5 40.8 %collective-permute-start = (bf16[1024,512]{1,0:T(8,128)(2,1)}, bf16[1024,512]{1,0:T(8,128)(2,1)S(1)}, u32[]{:S(2)}, u32[]{:S(2)}) collective-permute-start(bf16[1024,512]{1,0:T(8,128)(2,1)} %param.9), channel_id=1, source_target_pairs={{240,0},{0,16},{16,32},{32,48},{48,64},{64,80},{80,96},{96,112},{1... | collective-permute-start | bytes 3145736 | tf_op jit(solution)/shard_map/ppermute | solution.py:12
  17.3 30.4 %all-to-all-start = ((bf16[16,33,512]{2,1,0:T(8,128)(2,1)}), bf16[16,33,512]{2,1,0:T(8,128)(2,1)S(1)}, u32[]{:S(2)}, u32[]{:S(2)}) async-start(bf16[16,33,512]{2,1,0:T(8,128)(2,1)} %pad_maximum_fusion), calls=%async_computation | async-start | bytes 1310720 | tf_op jit(solution)/shard_map/all_to_all | solution.py:60
  28.2 54.3 %all-gather.3.cloned.1.call-start = ((), (), s32[]{:S(2)}) async-start(), calls=%async_computation.4 | async-start | bytes 3342336 | tf_op jit(solution)/shard_map/all_gather | solution.py:77
  48.3 78.3 %copy-start.1 = (bf16[1024,512]{1,0:T(8,128)(2,1)}, bf16[1024,512]{1,0:T(8,128)(2,1)S(1)}, u32[]{:S(2)}) copy-start(bf16[1024,512]{1,0:T(8,128)(2,1)S(1)} %collective-permute-done) | copy-start | bytes 3145732
  49.8 73.1 %all-gather.5.cloned.1.call-start = ((), (), s32[]{:S(2)}) async-start(), calls=%async_computation.5 | async-start | bytes 3342336 | tf_op jit(solution)/shard_map/all_gather | solution.py:78
  50.6 152.5 %reduce-scatter.3.cloned.1.call-start = ((), (), s32[]{:S(2)}) async-start(), calls=%async_computation.6 | async-start | bytes 3342336 | tf_op jit(solution)/shard_map/reduce_scatter | solution.py:95
  50.6 2.7 collective-permute-start.3
  122.9 3.7 %copy-start.5 = (bf16[1,192,8192]{2,1,0:T(8,128)(2,1)S(1)}, bf16[1,192,8192]{2,1,0:T(8,128)(2,1)}, u32[]{:S(2)}) copy-start(bf16[1,192,8192]{2,1,0:T(8,128)(2,1)} %param.14) | copy-start | bytes 9437188
  122.9 7.0 %copy-start.8 = (bf16[384,4096]{1,0:T(8,128)(2,1)S(1)}, bf16[384,4096]{1,0:T(8,128)(2,1)}, u32[]{:S(2)}) copy-start(bf16[384,4096]{1,0:T(8,128)(2,1)} %all-gather.5.cloned.1.call-done) | copy-start | bytes 9437188
  126.6 3.3 %copy-start.6 = (bf16[1,192,8192]{2,1,0:T(8,128)(2,1)S(1)}, bf16[1,192,8192]{2,1,0:T(8,128)(2,1)}, u32[]{:S(2)}) copy-start(bf16[1,192,8192]{2,1,0:T(8,128)(2,1)} %param.15) | copy-start | bytes 9437188
  129.9 1.9 copy-start.7
  131.8 1.9 copy-start
  136.4 2.9 copy-start.3
  136.4 135.2 %reduce-scatter.5.cloned.1.call-start = ((), (), s32[]{:S(2)}) async-start(), calls=%async_computation.7 | async-start | bytes 3342336 | tf_op jit(solution)/shard_map/reduce_scatter | solution.py:95
  139.3 143.6 %copy-start.4 = (s32[1,256]{1,0:T(1,128)S(1)}, s32[1,256]{1,0:T(1,128)}, u32[]{:S(2)}) copy-start(s32[1,256]{1,0:T(1,128)} %param.10) | copy-start | bytes 3076
  139.3 143.7 %copy-start.2 = (bf16[1024,512]{1,0:T(8,128)(2,1)S(1)}, bf16[1024,512]{1,0:T(8,128)(2,1)}, u32[]{:S(2)}) copy-start(bf16[1024,512]{1,0:T(8,128)(2,1)} %copy-done.1) | copy-start | bytes 3145732
  273.5 25.1 %all-to-all-start.1 = ((bf16[16,24,512]{2,1,0:T(8,128)(2,1)}), bf16[16,24,512]{2,1,0:T(8,128)(2,1)S(1)}, u32[]{:S(2)}, u32[]{:S(2)}) async-start(bf16[16,24,512]{2,1,0:T(8,128)(2,1)} %fusion.29), calls=%async_computation.3 | async-start | bytes 786432 | tf_op jit(solution)/shard_map/all_to_all | solution.py:107
Sparse Core Ops, SparseCore 0:
  49.9 32.5 all-gather.2
  84.3 38.5 all-gather.4
  136.5 66.4 reduce-scatter.2
  205.5 66.1 reduce-scatter.4
where the time goes:
time: 311 us; the launch traced here: 310 us
  waiting for transfers between devices  237 us (76%)
  starting transfers between devices  26.9 us (9%)
  matrix products  14.9 us (5%)
  between operations  13.5 us (4%)
  other arithmetic  10.8 us (3%)
  local copies, waits for them, and re-layouts  7.66 us (2%)
    reduce_scatter x2, waiting for transfers between devices, body(): lax.psum_scatter(lax.optimization_barrier(part.astype(jnp.bfloat16)).asty...  131 us
    all_gather x1, waiting for transfers between devices, body(): block_b = lax.all_gather(normed[:, half:], 'section', axis=0, tiled=True)  40.4 us
    all_gather x1, waiting for transfers between devices, body(): block_a = lax.all_gather(normed[:, :half], 'section', axis=0, tiled=True)  29.1 us
    all_to_all x1, waiting for transfers between devices, body(): lax.all_to_all(buffer, 'expert', split_axis=0, concat_axis=2, tiled=True)[0]  19.4 us
    all_to_all x1, waiting for transfers between devices, body(): lax.all_to_all(outgoing, 'expert', split_axis=0, concat_axis=0, tiled=True)  15.4 us
    all_to_all x1, starting transfers between devices, body(): lax.all_to_all(buffer, 'expert', split_axis=0, concat_axis=2, tiled=True)[0]  10.9 us
    dot_general x4, matrix products, feature_product(): lax.dot_general(block, weight, (((1,), (1,)), ((), ())), preferred_elemen...  9.33 us
    all_to_all x1, starting transfers between devices, body(): lax.all_to_all(outgoing, 'expert', split_axis=0, concat_axis=0, tiled=True)  9.06 us
  transfers between devices with their start and end apart: 10, of which 7 were waited for; matrix products, arithmetic and copies ran while one was open for 4% of the time, Pallas kernels for 0%

commit v1 on v0

--- a/solution.py
+++ b/solution.py
@@ -74,7 +74,10 @@
     score = jax.nn.sigmoid(scale * jnp.sum(picked * gains[None, :] * router_all[None, :], axis=1))
     score_home = passed_along(score, "section", 1)
     half = d // 2
-    block_a = lax.all_gather(normed[:, :half], "section", axis=0, tiled=True)
+    block_a = jnp.concatenate(
+        lax.all_to_all(jnp.stack([normed[:, :half]] * lax.axis_size("section")), "section", 0, 0),
+        axis=0,
+    )
     block_b = lax.all_gather(normed[:, half:], "section", axis=0, tiled=True)
     block_a, score_home = lax.optimization_barrier((block_a, score_home))
     gate = feature_product(block_a, gate_w[0, :, :half]) + feature_product(

time: 311 us -> 297 us (0.955)
  waiting for transfers between devices: 237 us -> 216 us
  starting transfers between devices: 26.9 us -> 32.3 us
    all_gather x1, waiting for transfers between devices: 40.4 us -> 5.64 us  [body(): block_b = lax.all_gather(normed[:, half:], 'section', axis=0, tiled=True)]
    all_gather x1 -> x0, waiting for transfers between devices: 29.1 us -> none  [body(): block_a = lax.all_gather(normed[:, :half], 'section', axis=0, tiled=True)]
    ppermute x4, waiting for transfers between devices: 0.73 us -> 27 us  [passed_along(): return lax.ppermute(block, axis, route)]
    all_to_all x0 -> x1, waiting for transfers between devices: none -> 19.2 us  [body(): lax.all_to_all(jnp.stack([normed[:, :half]] * lax.axis_size('section')),...]
    all_to_all x0 -> x1, starting transfers between devices: none -> 5.97 us  [body(): lax.all_to_all(jnp.stack([normed[:, :half]] * lax.axis_size('section')),...]
  transfers between devices with their start and end apart: 10 -> 10, of which waited for: 7 -> 7; matrix products, arithmetic and copies ran while one was open for 4% -> 5% of each run, Pallas kernels for 0% -> 0%
where the time goes in v1:
time: 297 us
  waiting for transfers between devices  216 us (73%)
  starting transfers between devices  32.3 us (11%)
  matrix products  14.5 us (5%)
  between operations  13.4 us (5%)
  other arithmetic  10.8 us (4%)
  local copies, waits for them, and re-layouts  9.43 us (3%)
    reduce_scatter x2, waiting for transfers between devices, body(): lax.psum_scatter(lax.optimization_barrier(part.astype(jnp.bfloat16)).asty...  129 us
    ppermute x4, waiting for transfers between devices, passed_along(): return lax.ppermute(block, axis, route)  27 us
    all_to_all x1, waiting for transfers between devices, body(): lax.all_to_all(buffer, 'expert', split_axis=0, concat_axis=2, tiled=True)[0]  19.4 us
    all_to_all x1, waiting for transfers between devices, body(): lax.all_to_all(jnp.stack([normed[:, :half]] * lax.axis_size('section')),...  19.2 us
    all_to_all x1, waiting for transfers between devices, body(): lax.all_to_all(outgoing, 'expert', split_axis=0, concat_axis=0, tiled=True)  15.4 us
    all_to_all x1, starting transfers between devices, body(): lax.all_to_all(buffer, 'expert', split_axis=0, concat_axis=2, tiled=True)[0]  10.9 us
    all_to_all x1, starting transfers between devices, body(): lax.all_to_all(outgoing, 'expert', split_axis=0, concat_axis=0, tiled=True)  9.03 us
    dot_general x4, matrix products, feature_product(): lax.dot_general(block, weight, (((1,), (1,)), ((), ())), preferred_elemen...  7.3 us
  transfers between devices with their start and end apart: 10, of which 7 were waited for; matrix products, arithmetic and copies ran while one was open for 5% of the time, Pallas kernels for 0%

profile of v1, /device:TPU:7, one launch (start us, length us, event | category | flops | bytes accessed | tf_op | source)
XLA Modules:
  0.0 296.6 jit_solution(16365952748406818884)
XLA Ops:
  6.5 0.7 collective-permute-start.1
  7.2 0.3 collective-permute-start.2
  7.5 3.6 %collective-permute-start = (bf16[1024,512]{1,0:T(8,128)(2,1)}, bf16[1024,512]{1,0:T(8,128)(2,1)S(1)}, u32[]{:S(2)}, u32[]{:S(2)}) collective-permute-start(bf16[1024,512]{1,0:T(8,128)(2,1)} %param.9), channel_id=1, source_target_pairs={{240,0},{0,16},{16,32},{32,48},{48,64},{64,80},{80,96},{96,112},{1... | collective-permute-start | bytes 3145736 | tf_op jit(solution)/shard_map/ppermute | solution.py:12
  11.1 0.7 fusion.38
  11.8 0.7 fusion.37
  12.5 0.0 collective-permute-done.1
  12.5 0.6 reduce-window.14
  13.1 0.2 slice_reduce_fusion.1
  13.4 0.1 fusion.34
  13.5 0.0 collective-permute-done.2
  13.5 2.6 gather_fusion
  16.1 0.3 convolution_convert_fusion.2
  16.4 0.9 pad_maximum_fusion
  17.3 10.9 %all-to-all-start = ((bf16[16,33,512]{2,1,0:T(8,128)(2,1)}), bf16[16,33,512]{2,1,0:T(8,128)(2,1)S(1)}, u32[]{:S(2)}, u32[]{:S(2)}) async-start(bf16[16,33,512]{2,1,0:T(8,128)(2,1)} %pad_maximum_fusion), calls=%async_computation | async-start | bytes 1310720 | tf_op jit(solution)/shard_map/all_to_all | solution.py:60
  28.2 0.0 all-gather.2.cloned.1.call-start
  28.2 19.4 %all-to-all-done = bf16[16,33,512]{2,1,0:T(8,128)(2,1)S(1)} async-done(((bf16[16,33,512]{2,1,0:T(8,128)(2,1)}), bf16[16,33,512]{2,1,0:T(8,128)(2,1)S(1)}, u32[]{:S(2)}, u32[]{:S(2)}) %all-to-all-start) | async-done | bytes 540704 | tf_op jit(solution)/shard_map/all_to_all | solution.py:60
  47.6 0.2 copy.34
  47.8 0.1 pad.13
  47.9 0.4 copy.28
  48.3 0.0 collective-permute-done
  48.3 0.0 copy-start.1
  48.3 0.1 slice_add_fusion
  48.5 0.3 fusion.26
  48.8 0.2 fusion.24
  49.0 0.7 fusion.40
  49.7 0.0 all-gather.2.cloned.1.call-update
  49.7 2.1 stack.2
  51.8 0.0 copy-done.1
  51.8 6.0 %all-to-all-start.1 = ((bf16[16,24,4096]{2,1,0:T(8,128)(2,1)}), bf16[16,24,4096]{2,1,0:T(8,128)(2,1)S(1)}, u32[]{:S(2)}, u32[]{:S(2)}) async-start(bf16[16,24,4096]{2,1,0:T(8,128)(2,1)} %stack.2), calls=%async_computation.1 | async-start | bytes 6291456 | tf_op jit(solution)/shard_map/all_to_all | solution.py:78
  57.8 0.0 reduce-scatter.5.cloned.1.call-start
  57.8 1.5 collective-permute-start.3
  59.3 27.0 %collective-permute-done.3 = f32[24]{0:T(128)S(1)} collective-permute-done((f32[24]{0:T(128)S(1)}, f32[24]{0:T(128)S(1)}, u32[]{:S(2)}, u32[]{:S(2)}) %collective-permute-start.3) | collective-permute-done | bytes 128 | tf_op jit(solution)/shard_map/ppermute | solution.py:12
  86.3 19.2 %all-to-all-done.1 = bf16[16,24,4096]{2,1,0:T(8,128)(2,1)S(1)} async-done(((bf16[16,24,4096]{2,1,0:T(8,128)(2,1)}), bf16[16,24,4096]{2,1,0:T(8,128)(2,1)S(1)}, u32[]{:S(2)}, u32[]{:S(2)}) %all-to-all-start.1) | async-done | bytes 3145760 | tf_op jit(solution)/shard_map/all_to_all | solution.py:78
  105.5 5.6 %all-gather.2.cloned.1.call-done = bf16[384,4096]{1,0:T(8,128)(2,1)} async-done(((bf16[24,4096]{1,0:T(8,128)(2,1)}), bf16[384,4096]{1,0:T(8,128)(2,1)}) %all-gather.2.cloned.1.call-update) | async-done | bytes 3145744 | tf_op jit(solution)/shard_map/all_gather | solution.py:81
  111.2 3.7 %fusion.6 = f32[384,192]{0,1:T(8,128)S(1)} fusion(bf16[384,4096]{1,0:T(8,128)(2,1)} %all-gather.2.cloned.1.call-done, bf16[1,192,8192]{2,1,0:T(8,128)(2,1)} %param.14), kind=kOutput, calls=%fused_computation.11 | convolution fusion | flops 603979776 | bytes 5013504 | tf_op jit(solution)/shard_map/dot_general | solution.py:16
  114.9 0.0 copy-start.6
  114.9 1.2 fusion.16
  116.1 0.8 copy-done.6
  116.9 1.2 fusion.2
  118.1 1.2 multiply_convert_fusion.1
  119.3 0.1 slice_bitcast_fusion
  119.4 0.1 copy.19
  119.6 0.1 copy.20
  119.6 0.1 pad_maximum_fusion.1
  119.7 0.0 copy-start
  119.7 4.2 %convolution_convert_fusion = bf16[384,4096]{1,0:T(8,128)(2,1)} fusion(bf16[384,192]{1,0:T(8,128)(2,1)S(1)} %bitcast.108, bf16[1,192,8192]{2,1,0:T(8,128)(2,1)} %param.16), kind=kOutput, calls=%fused_computation.3 | convolution fusion | flops 605552640 | bytes 4866048 | tf_op jit(solution)/shard_map/dot_general | solution.py:96
  123.9 0.0 reduce-scatter.5.cloned.1.call-update
  123.9 0.0 copy-start.3
  123.9 0.2 reduce-scatter.3.cloned.1.call-start
  124.2 2.7 convolution_convert_fusion.1
  126.9 0.0 reduce-scatter.3.cloned.1.call-update
  126.9 0.6 reduce-window.16
  127.5 61.7 %reduce-scatter.5.cloned.1.call-done = bf16[24,4096]{1,0:T(8,128)(2,1)} async-done(((bf16[384,4096]{1,0:T(8,128)(2,1)}), bf16[24,4096]{1,0:T(8,128)(2,1)}) %reduce-scatter.5.cloned.1.call-update) | async-done | bytes 196624 | tf_op jit(solution)/shard_map/reduce_scatter | solution.py:98
  189.2 0.9 copy.35
  190.1 67.8 %reduce-scatter.3.cloned.1.call-done = bf16[24,4096]{1,0:T(8,128)(2,1)} async-done(((bf16[384,4096]{1,0:T(8,128)(2,1)}), bf16[24,4096]{1,0:T(8,128)(2,1)}) %reduce-scatter.3.cloned.1.call-update) | async-done | bytes 196624 | tf_op jit(solution)/shard_map/reduce_scatter | solution.py:98
  257.9 0.9 copy.36
  258.9 0.9 fusion.29
  259.8 9.0 %all-to-all-start.2 = ((bf16[16,24,512]{2,1,0:T(8,128)(2,1)}), bf16[16,24,512]{2,1,0:T(8,128)(2,1)S(1)}, u32[]{:S(2)}, u32[]{:S(2)}) async-start(bf16[16,24,512]{2,1,0:T(8,128)(2,1)} %fusion.29), calls=%async_computation.4 | async-start | bytes 786432 | tf_op jit(solution)/shard_map/all_to_all | solution.py:110
  268.9 0.2 slice_reduce_fusion
  269.1 0.1 fusion.32
  269.2 0.3 convert_element_type.78
  269.5 15.4 %all-to-all-done.2 = bf16[16,24,512]{2,1,0:T(8,128)(2,1)S(1)} async-done(((bf16[16,24,512]{2,1,0:T(8,128)(2,1)}), bf16[16,24,512]{2,1,0:T(8,128)(2,1)S(1)}, u32[]{:S(2)}, u32[]{:S(2)}) %all-to-all-start.2) | async-done | bytes 393248 | tf_op jit(solution)/shard_map/all_to_all | solution.py:110
  284.9 4.0 %scatter_custom_fusion = f32[1024,512]{1,0:T(8,128)S(1)} fusion(f32[1024,512]{1,0:T(8,128)S(1)} %convert_element_type.78, s32[256]{0:T(256)S(1)} %bitcast.134, bf16[384,512]{1,0:T(8,128)(2,1)S(1)} %bitcast.113, s32[1024]{0:T(1024)S(1)} %pad_clamp_fusion), kind=kCustom, calls=%fused_computation.35 | custom fusion | flops 262144 | bytes 2494464 | tf_op jit(solution)/shard_map/scatter-add | solution.py:116
  288.9 1.1 convert_element_type.90
  (29 shorter events, 0.3 us)
Async XLA Ops:
  6.5 6.0 %collective-permute-start.1 = (s32[256,1]{0,1:T(1,128)}, s32[256,1]{0,1:T(1,128)S(1)}, u32[]{:S(2)}, u32[]{:S(2)}) collective-permute-start(s32[256,1]{0,1:T(1,128)} %param.11), channel_id=1, source_target_pairs={{16,0},{32,16},{48,32},{64,48},{80,64},{96,80},{112,96},{128,112},... | collective-permute-start | bytes 3080 | tf_op jit(solution)/shard_map/ppermute | solution.py:12
  7.2 6.2 %collective-permute-start.2 = (s32[1,256]{1,0:T(1,128)}, s32[1,256]{1,0:T(1,128)S(1)}, u32[]{:S(2)}, u32[]{:S(2)}) collective-permute-start(s32[1,256]{1,0:T(1,128)} %param.10), channel_id=1, source_target_pairs={{16,0},{32,16},{48,32},{64,48},{80,64},{96,80},{112,96},{128,112},... | collective-permute-start | bytes 3080 | tf_op jit(solution)/shard_map/ppermute | solution.py:12
  7.5 40.8 %collective-permute-start = (bf16[1024,512]{1,0:T(8,128)(2,1)}, bf16[1024,512]{1,0:T(8,128)(2,1)S(1)}, u32[]{:S(2)}, u32[]{:S(2)}) collective-permute-start(bf16[1024,512]{1,0:T(8,128)(2,1)} %param.9), channel_id=1, source_target_pairs={{240,0},{0,16},{16,32},{32,48},{48,64},{64,80},{80,96},{96,112},{1... | collective-permute-start | bytes 3145736 | tf_op jit(solution)/shard_map/ppermute | solution.py:12
  17.3 30.4 %all-to-all-start = ((bf16[16,33,512]{2,1,0:T(8,128)(2,1)}), bf16[16,33,512]{2,1,0:T(8,128)(2,1)S(1)}, u32[]{:S(2)}, u32[]{:S(2)}) async-start(bf16[16,33,512]{2,1,0:T(8,128)(2,1)} %pad_maximum_fusion), calls=%async_computation | async-start | bytes 1310720 | tf_op jit(solution)/shard_map/all_to_all | solution.py:60
  28.2 83.0 %all-gather.2.cloned.1.call-start = ((), (), s32[]{:S(2)}) async-start(), calls=%async_computation.5 | async-start | bytes 3342336 | tf_op jit(solution)/shard_map/all_gather | solution.py:81
  48.3 3.5 %copy-start.1 = (bf16[1024,512]{1,0:T(8,128)(2,1)}, bf16[1024,512]{1,0:T(8,128)(2,1)S(1)}, u32[]{:S(2)}) copy-start(bf16[1024,512]{1,0:T(8,128)(2,1)S(1)} %collective-permute-done) | copy-start | bytes 3145732
  51.8 53.7 %all-to-all-start.1 = ((bf16[16,24,4096]{2,1,0:T(8,128)(2,1)}), bf16[16,24,4096]{2,1,0:T(8,128)(2,1)S(1)}, u32[]{:S(2)}, u32[]{:S(2)}) async-start(bf16[16,24,4096]{2,1,0:T(8,128)(2,1)} %stack.2), calls=%async_computation.1 | async-start | bytes 6291456 | tf_op jit(solution)/shard_map/all_to_all | solution.py:78
  57.8 131.4 %reduce-scatter.5.cloned.1.call-start = ((), (), s32[]{:S(2)}) async-start(), calls=%async_computation.7 | async-start | bytes 3342336 | tf_op jit(solution)/shard_map/reduce_scatter | solution.py:98
  57.8 28.5 %collective-permute-start.3 = (f32[24]{0:T(128)S(1)}, f32[24]{0:T(128)S(1)}, u32[]{:S(2)}, u32[]{:S(2)}) collective-permute-start(f32[24]{0:T(128)S(1)} %get-tuple-element.19), channel_id=1, source_target_pairs={{240,0},{0,16},{16,32},{32,48},{48,64},{64,80},{80,96},{96,112},{1... | collective-permute-start | bytes 296 | tf_op jit(solution)/shard_map/ppermute | solution.py:12
  111.2 3.7 %copy-start.5 = (bf16[1,192,8192]{2,1,0:T(8,128)(2,1)S(1)}, bf16[1,192,8192]{2,1,0:T(8,128)(2,1)}, u32[]{:S(2)}) copy-start(bf16[1,192,8192]{2,1,0:T(8,128)(2,1)} %param.14) | copy-start | bytes 9437188
  111.2 4.9 %copy-start.7 = (bf16[384,4096]{1,0:T(8,128)(2,1)S(1)}, bf16[384,4096]{1,0:T(8,128)(2,1)}, u32[]{:S(2)}) copy-start(bf16[384,4096]{1,0:T(8,128)(2,1)} %all-gather.2.cloned.1.call-done) | copy-start | bytes 9437188
  114.9 2.0 copy-start.6
  119.7 4.5 %copy-start = (bf16[1,192,8192]{2,1,0:T(8,128)(2,1)S(1)}, bf16[1,192,8192]{2,1,0:T(8,128)(2,1)}, u32[]{:S(2)}) copy-start(bf16[1,192,8192]{2,1,0:T(8,128)(2,1)} %param.16) | copy-start | bytes 9437188
  123.9 3.0 %copy-start.3 = (s32[256,1]{0,1:T(1,128)S(1)}, s32[256,1]{0,1:T(1,128)}, u32[]{:S(2)}) copy-start(s32[256,1]{0,1:T(1,128)} %param.11) | copy-start | bytes 3076
  123.9 134.0 %reduce-scatter.3.cloned.1.call-start = ((), (), s32[]{:S(2)}) async-start(), calls=%async_computation.6 | async-start | bytes 3342336 | tf_op jit(solution)/shard_map/reduce_scatter | solution.py:98
  126.9 142.3 %copy-start.4 = (s32[1,256]{1,0:T(1,128)S(1)}, s32[1,256]{1,0:T(1,128)}, u32[]{:S(2)}) copy-start(s32[1,256]{1,0:T(1,128)} %param.10) | copy-start | bytes 3076
  126.9 142.4 %copy-start.2 = (bf16[1024,512]{1,0:T(8,128)(2,1)S(1)}, bf16[1024,512]{1,0:T(8,128)(2,1)}, u32[]{:S(2)}) copy-start(bf16[1024,512]{1,0:T(8,128)(2,1)} %copy-done.1) | copy-start | bytes 3145732
  259.8 25.1 %all-to-all-start.2 = ((bf16[16,24,512]{2,1,0:T(8,128)(2,1)}), bf16[16,24,512]{2,1,0:T(8,128)(2,1)S(1)}, u32[]{:S(2)}, u32[]{:S(2)}) async-start(bf16[16,24,512]{2,1,0:T(8,128)(2,1)} %fusion.29), calls=%async_computation.4 | async-start | bytes 786432 | tf_op jit(solution)/shard_map/all_to_all | solution.py:110
Sparse Core Ops, SparseCore 0:
  49.8 61.2 all-gather.1
  124.0 65.0 reduce-scatter.4
  191.7 66.1 reduce-scatter.2
